TPU v7x, 256 devices: a whole 4x4x8 slice. The times are simulated.
256 devices in a mesh: dp: 16 (over x, z_lo, core), space: 16 (over y, z_hi).
Axes of the slice: x: 4, y: 4, z: 8 (z_hi: 4, z_lo: 2; z = z_hi * 2 + z_lo), core: 2. Of those that a mesh axis runs over, the one named last changes fastest.
Arguments:
- acts_in: bfloat16 [16, 64, 64, 32, 128], P('dp', 'space'), may hold values from -6 to 6
- pre_act: bfloat16 [16, 64, 64, 32, 128], P('dp', 'space'), may hold values from -6 to 6
- weight_two: bfloat16 [128, 3, 3, 3, 128], P('space'), may hold values from -0.109375 to 0.109375
- grad_out: bfloat16 [16, 32, 32, 16, 128], P('dp', None, None, None, 'space'), may hold values from -6 to 6
Outputs:
- fine_grad: float32 [128, 3, 3, 3, 128], P('space')
- coarse_grad: float32 [128, 3, 3, 3, 128], P('space')
All inputs are finite; a program needn't handle non-finite values.
Results may differ from a plain program's by a relative error of at most 0.003.
Values may be sent and summed in bfloat16 or wider, within the bound.
No kernel may reach another device: no remote copies, remote signals or barrier semaphores. Data moves between devices by JAX's collectives and lax.ppermute only.
A program may use at most 128 MiB of HBM per device.

v0:
```python
import math
import jax
import jax.numpy as jnp
from jax import lax
from jax.sharding import PartitionSpec as P

leak_slope = 0.3
parity_taps = {0: ((1, 0),), 1: ((0, 1), (2, 0))}


def passed_along(block, axis, distance):
    devices = range(lax.axis_size(axis))
    route = [(i - distance, i) for i in devices if i - distance in devices]
    return lax.ppermute(block, axis, route)


def padded_2(shard, sides, width):
    for axis, dim in sides:
        size, length = (lax.axis_size(axis), shard.shape[dim])
        up = [(i, (i + 1) % size) for i in range(size - 1)]
        down = [(j, i) for i, j in up]
        last = lax.slice_in_dim(shard, length - width, length, axis=dim)
        initial = lax.slice_in_dim(shard, 0, width, axis=dim)
        before = lax.ppermute(last, axis, up)
        after = lax.ppermute(initial, axis, down)
        shard = jnp.concatenate([before, shard, after], axis=dim)
    return shard


def transpose_conv(padded, weight):
    rows_x = padded.shape[0] - 1
    rows_y = padded.shape[1] - 1
    rows_z = padded.shape[2] - 1
    outputs = weight.shape[4]
    zpair = jnp.concatenate([padded[:, :, :rows_z, :], padded[:, :, 1:, :]], axis=3)
    nothing = jnp.zeros((weight.shape[0], outputs), weight.dtype)
    classes = []
    for parity_x in (0, 1):
        for parity_y in (0, 1):
            pieces = []
            blocks = []
            for tap_x, move_x in parity_taps[parity_x]:
                for tap_y, move_y in parity_taps[parity_y]:
                    pieces.append(zpair[move_x : move_x + rows_x, move_y : move_y + rows_y])
                    taps = weight[:, tap_x, tap_y]
                    first = jnp.concatenate([taps[:, 1], taps[:, 2]], axis=1)
                    second = jnp.concatenate([nothing, taps[:, 0]], axis=1)
                    blocks.append(jnp.concatenate([first, second], axis=0))
            stacked = jnp.concatenate(pieces, axis=3)
            flat = stacked.reshape(-1, stacked.shape[3])
            mixing = jnp.concatenate(blocks, axis=0)
            classes.append(jnp.dot(flat, mixing, preferred_element_type=jnp.float32))
    joined = jnp.stack(classes).reshape(2, 2, rows_x, rows_y, rows_z, 2 * outputs)
    joined = joined.transpose(2, 0, 3, 1, 4, 5)
    return joined.reshape(2 * rows_x, 2 * rows_y, 2 * rows_z, outputs)


def depth_taps(volume):
    count_x, count_y, count_z, channels = volume.shape
    paired = volume.reshape(count_x, count_y, count_z // 2, 2 * channels)
    even = paired[..., :channels]
    odd = paired[..., channels:]
    earlier = jnp.pad(odd[:, :, :-1, :], ((0, 0), (0, 0), (1, 0), (0, 0)))
    return jnp.concatenate([earlier, even, odd], axis=3)


def coarse_terms(hidden, below, gradient):
    count_x, count_y, count_z, filters = gradient.shape
    flat_grad = gradient.reshape(-1, filters)
    stacked = depth_taps(hidden)
    width = stacked.shape[3]
    split = stacked.reshape(count_x, 2, count_y, 2, count_z, width)
    rim = depth_taps(below).reshape(1, count_y, 2, count_z, width)
    by_x = [jnp.concatenate([rim, split[:-1, 1]], axis=0), split[:, 0], split[:, 1]]
    terms = []
    for tap_x in range(3):
        plane = by_x[tap_x]
        by_y = [
            jnp.pad(plane[:, :-1, 1], ((0, 0), (1, 0), (0, 0), (0, 0))),
            plane[:, :, 0],
            plane[:, :, 1],
        ]
        for tap_y in range(3):
            piece = by_y[tap_y].reshape(-1, width)
            terms.append(
                lax.dot_general(
                    flat_grad, piece, (((0,), (0,)), ((), ())), preferred_element_type=jnp.float32
                )
            )
    return jnp.stack(terms, axis=1).reshape(filters, 3, 3, 3, width // 3)


def fine_terms(framed, gradient):
    count_x, count_y, count_z, filters = gradient.shape
    flat_grad = gradient.reshape(-1, filters)
    stacked = jnp.concatenate(
        [framed[:, :, shift : shift + count_z, :] for shift in range(3)], axis=3
    )
    width = stacked.shape[3]
    terms = []
    for tap_x in range(3):
        for tap_y in range(3):
            piece = stacked[tap_x : tap_x + count_x, tap_y : tap_y + count_y].reshape(-1, width)
            terms.append(
                lax.dot_general(
                    flat_grad, piece, (((0,), (0,)), ((), ())), preferred_element_type=jnp.float32
                )
            )
    return jnp.stack(terms, axis=1).reshape(filters, 3, 3, 3, width // 3)


def filter_share(whole_terms):
    return lax.psum_scatter(whole_terms, "space", scatter_dimension=0, tiled=True)


def body(acts_in, pre_act, weight_two, grad_out):
    parts = lax.axis_size("space")
    groups = lax.axis_size("dp")
    acts = acts_in[0]
    depth, across, height, channels = acts.shape
    scaling = 1.0 / math.sqrt(groups * depth * parts * across * height)
    before_f = pre_act[0].astype(jnp.float32)
    hidden = jnp.where(before_f > 0, before_f, leak_slope * before_f).astype(jnp.bfloat16)
    grad_tile = lax.all_to_all(grad_out, "space", split_axis=1, concat_axis=4, tiled=True)[0]
    below = passed_along(hidden[-1:], "space", 1)
    whole_weight = lax.all_gather(weight_two, "space", axis=0, tiled=True)
    above = passed_along(grad_tile[:1], "space", -1)
    upper = jnp.pad(jnp.concatenate([grad_tile, above], axis=0), ((0, 0), (0, 1), (0, 1), (0, 0)))
    back = transpose_conv(upper, whole_weight)
    delta = (back * jnp.where(before_f > 0, 1.0, leak_slope)).astype(jnp.bfloat16)
    framed = padded_2(acts, (("space", 0),), 1)
    framed = jnp.pad(framed, ((0, 0), (1, 1), (1, 1), (0, 0)))
    coarse_full = coarse_terms(hidden, below, grad_tile)
    fine_full = fine_terms(framed, delta)
    coarse_all, fine_all = lax.psum((coarse_full, fine_full), "dp")
    coarse_sum = filter_share(coarse_all)
    fine_sum = filter_share(fine_all)
    return (fine_sum * scaling, coarse_sum * scaling)


def solution(mesh):
    placed = (
        P("dp", "space", None, None, None),
        P("dp", "space", None, None, None),
        P("space", None, None, None, None),
        P("dp", None, None, None, "space"),
    )
    return jax.shard_map(
        body,
        mesh=mesh,
        in_specs=placed,
        out_specs=(P("space", None, None, None, None), P("space", None, None, None, None)),
        check_vma=False,
    )
```

profile of v0, /device:TPU:1, one launch (start us, length us, event | category | flops | bytes accessed | tf_op | source)
XLA Modules:
  0.0 557.8 jit_solution(2859011999417366187)
XLA Ops:
  10.2 11.7 %all-to-all-start = ((bf16[16,2,4096]{2,1,0:T(2,128)(2,1)}), bf16[16,2,4096]{2,1,0:T(2,128)(2,1)S(1)}, u32[]{:S(2)}, u32[]{:S(2)}) async-start(bf16[16,2,4096]{2,1,0:T(2,128)(2,1)} %reshape.94), calls=%async_computation | async-start | bytes 524288 | tf_op jit(solution)/shard_map/all_to_all | solution.py:124
  22.0 2.3 slice_bitcast_fusion.7
  24.3 5.0 collective-permute-start.1
  30.5 2.7 reshape.82
  33.2 2.8 fusion.22
  40.5 51.2 %all_gather.3 = bf16[128,3,3,3,128]{4,0,3,2,1:T(8,128)(2,1)S(1)} all-gather(bf16[8,3,3,3,128]{4,0,3,2,1:T(8,128)(2,1)S(1)} %copy-done.13), channel_id=1, replica_groups=mesh['dp'=16,'space'=16] {'space'}, dimensions={0}, use_global_device_ids=true | all-gather | bytes 940032 | tf_op jit(solution)/shard_map/all_gather | solution.py:126
  100.8 2.6 convert_bitcast_fusion
  105.1 3.6 reshape_squeeze.21
  111.8 2.8 copy.55
  114.5 4.6 select_maximum_fusion
  119.1 3.8 fusion.164
  122.9 8.0 %pad_maximum_fusion = bf16[6,66,32,384]{3,2,1,0:T(8,128)(2,1)} fusion(bf16[6,66,32,128]{3,2,1,0:T(8,128)(2,1)} %get-tuple-element.16, bf16[6,66,32,128]{3,2,1,0:T(8,128)(2,1)} %get-tuple-element.15, bf16[6,66,32,128]{3,2,1,0:T(8,128)(2,1)S(1)} %get-tuple-element.14), kind=kLoop, calls=%fused_computation.5 | loop fusion | flops 29196288 | bytes 19464192 | tf_op jit(solution)/shard_map/concatenate | solution.py:96
  139.6 2.6 copy.57
  142.2 4.9 reshape.73
  147.1 3.4 multiply_convert_fusion
  151.9 4.7 collective-permute-start.3
  156.7 4.9 fusion.45
  163.6 2.0 fusion.57
  165.6 2.0 fusion.63
  177.4 2.3 copy.58
  179.6 2.5 copy.59
  187.7 2.5 copy.60
  192.2 234.4 %all-reduce.23.cloned.1.call-done = (f32[128,3,3,3,128]{4,3,2,1,0:T(4,128)}, f32[128,3,3,3,128]{4,3,2,1,0:T(4,128)}) async-done(((f32[128,3,3,3,128]{4,3,2,1,0:T(4,128)}, f32[128,3,3,3,128]{4,3,2,1,0:T(4,128)}), (f32[128,3,3,3,128]{4,3,2,1,0:T(4,128)}, f32[128,3,3,3,128]{4,3,2,1,0:T(4,128)})) %all-reduce.23.cloned.1.call-update) | async-done | bytes 3538960
  429.9 117.9 %all-reduce.25.cloned.1.call-done = (f32[8,3,3,3,128]{4,3,2,1,0:T(4,128)}, f32[8,3,3,3,128]{4,3,2,1,0:T(4,128)}) async-done(((f32[8,3,3,3,128]{4,3,2,1,0:T(4,128)}, f32[8,3,3,3,128]{4,3,2,1,0:T(4,128)}), (f32[8,3,3,3,128]{4,3,2,1,0:T(4,128)}, f32[8,3,3,3,128]{4,3,2,1,0:T(4,128)})) %all-reduce.25.cloned.1.call-update) | async-done | bytes 221200 | tf_op jit(solution)/shard_map/psum | solution.py:135
  (142 shorter events, 57.2 us)
Async XLA Ops:
  8.5 22.0 %copy-start.2 = (bf16[1,4,64,32,128]{4,3,2,1,0:T(8,128)(2,1)S(1)}, bf16[1,4,64,32,128]{4,3,2,1,0:T(8,128)(2,1)}, u32[]{:S(2)}) copy-start(bf16[1,4,64,32,128]{4,3,2,1,0:T(8,128)(2,1)} %param.5) | copy-start | bytes 6291460
  10.2 93.2 %all-to-all-start = ((bf16[16,2,4096]{2,1,0:T(2,128)(2,1)}), bf16[16,2,4096]{2,1,0:T(2,128)(2,1)S(1)}, u32[]{:S(2)}, u32[]{:S(2)}) async-start(bf16[16,2,4096]{2,1,0:T(2,128)(2,1)} %reshape.94), calls=%async_computation | async-start | bytes 524288 | tf_op jit(solution)/shard_map/all_to_all | solution.py:124
  22.0 404.7 %all-reduce.23.cloned.1.call-start = ((), (), s32[]{:S(2)}) async-start(), calls=%async_computation.1 | async-start | bytes 9437184
  24.3 90.2 %collective-permute-start.1 = (bf16[1,64,32,128]{3,2,1,0:T(8,128)(2,1)}, bf16[1,64,32,128]{3,2,1,0:T(8,128)(2,1)}, u32[]{:S(2)}, u32[]{:S(2)}) collective-permute-start(bf16[1,64,32,128]{3,2,1,0:T(8,128)(2,1)} %get-tuple-element.19), channel_id=1, source_target_pairs={{0,1},{1,2},{2,3},{3,4},{4,5},{5,6},{6,7},{7,8},{8,9},{9,10},{10,1... | collective-permute-start | bytes 1572872 | tf_op jit(solution)/shard_map/ppermute | solution.py:24
  29.2 85.3 %collective-permute-start.2 = (bf16[1,64,32,128]{3,2,1,0:T(8,128)(2,1)}, bf16[1,64,32,128]{3,2,1,0:T(8,128)(2,1)}, u32[]{:S(2)}, u32[]{:S(2)}) collective-permute-start(bf16[1,64,32,128]{3,2,1,0:T(8,128)(2,1)} %get-tuple-element.20), channel_id=1, source_target_pairs={{1,0},{2,1},{3,2},{4,3},{5,4},{6,5},{7,6},{8,7},{9,8},{10,9},{11,1... | collective-permute-start | bytes 1572872 | tf_op jit(solution)/shard_map/ppermute | solution.py:25
  38.7 1.8 copy-start.13
  110.3 22.4 %collective-permute-start = (bf16[1,32,16,128]{1,3,2,0:T(8,128)(2,1)}, bf16[1,32,16,128]{1,3,2,0:T(8,128)(2,1)}, u32[]{:S(2)}, u32[]{:S(2)}) collective-permute-start(bf16[1,32,16,128]{1,3,2,0:T(8,128)(2,1)} %bitcast.329), channel_id=1, source_target_pairs={{1,0},{2,1},{3,2},{4,3},{5,4},{6,5},{7,6},{8,7},{9,8},{10,9},{11,1... | collective-permute-start | bytes 393224 | tf_op jit(solution)/shard_map/ppermute | solution.py:14
  135.9 1.9 copy-start.11
  135.9 1.9 copy-start.12
  135.9 2.3 copy-start.14
  135.9 2.3 copy-start.15
  135.9 2.3 copy-start.16
  136.0 2.3 copy-start.17
  136.0 2.3 copy-start.18
  136.0 2.3 copy-start.19
  142.2 4.9 copy-start.3
  147.1 14.5 %slice-start = ((s8[9732096]{0:T(1024)(128)(4,1)}), s8[1343488]{0:T(1024)(128)(4,1)S(1)}, s32[]{:S(2)}) async-start(s8[9732096]{0:T(1024)(128)(4,1)} %bitcast.309), calls=%async_computation.3 | async-start | bytes 2686976
  147.1 14.5 %slice-start.1 = ((s8[9732096]{0:T(1024)(128)(4,1)}), s8[4194304]{0:T(1024)(128)(4,1)S(1)}, s32[]{:S(2)}) async-start(s8[9732096]{0:T(1024)(128)(4,1)} %bitcast.309), calls=%async_computation.4 | async-start | bytes 8388608
  151.9 30.2 %collective-permute-start.3 = (bf16[1,64,32,128]{3,2,1,0:T(8,128)(2,1)S(1)}, bf16[1,64,32,128]{3,2,1,0:T(8,128)(2,1)S(1)}, u32[]{:S(2)}, u32[]{:S(2)}) collective-permute-start(bf16[1,64,32,128]{3,2,1,0:T(8,128)(2,1)S(1)} %fusion.96), channel_id=1, source_target_pairs={{0,1},{1,2},{2,3},{3,4},{4,5},{5,6},{6,7},{7,8},{8,9},{9,10},{10,1... | collective-permute-start | bytes 1572872 | tf_op jit(solution)/shard_map/ppermute | solution.py:14
  156.6 4.9 slice-start.2
  184.2 1.8 copy-start.6
  184.7 1.8 copy-start.8
  190.2 360.7 %copy-start.1 = (bf16[1,32,32,16,8]{2,4,3,1,0:T(8,128)(2,1)S(1)}, bf16[1,32,32,16,8]{2,4,3,1,0:T(8,128)(2,1)}, u32[]{:S(2)}) copy-start(bf16[1,32,32,16,8]{2,4,3,1,0:T(8,128)(2,1)} %param.7) | copy-start | bytes 786436
  190.3 357.5 %all-reduce.25.cloned.1.call-start = ((), (), s32[]{:S(2)}) async-start(), calls=%async_computation.2 | async-start | bytes 589824 | tf_op jit(solution)/shard_map/psum | solution.py:135
  (13 other events, 14.9 us)
Sparse Core Ops, SparseCore 0:
  190.4 236.2 all-reduce.22
  430.0 117.7 all-reduce.24
where the time goes:
time: 559 us; the launch traced here: 558 us
  waiting for transfers between devices  354 us (63%)
  local copies, waits for them, and re-layouts  54.9 us (10%)
  blocking collectives  51.2 us (9%)
  other arithmetic  30.5 us (5%)
  matrix products  27.4 us (5%)
  starting transfers between devices  24.2 us (4%)
  between operations  15.4 us (3%)
    unnamed x3, waiting for transfers between devices  234 us
    psum x1, waiting for transfers between devices, body(): coarse_all, fine_all = lax.psum((coarse_full, fine_full), 'dp')  118 us
    all_gather x1, blocking collectives, body(): whole_weight = lax.all_gather(weight_two, 'space', axis=0, tiled=True)  51.2 us
    dot_general x9, matrix products, fine_terms(): lax.dot_general(flat_grad, piece, (((0,), (0,)), ((), ())), preferred_ele...  20.7 us
    unnamed x71, local copies, waits for them, and re-layouts  11.9 us
    all_to_all x1, starting transfers between devices, body(): lax.all_to_all(grad_out, 'space', split_axis=1, concat_axis=4, tiled=True)  11.7 us
  transfers between devices with their start and end apart: 7, of which 3 were waited for; matrix products, arithmetic and copies ran while one was open for 14% of the time, Pallas kernels for 0%

commit v1 on v0

--- a/solution.py
+++ b/solution.py
@@ -1,3 +1,4 @@
+import functools
 import math
 import jax
 import jax.numpy as jnp
@@ -6,6 +7,16 @@
 
 leak_slope = 0.3
 parity_taps = {0: ((1, 0),), 1: ((0, 1), (2, 0))}
+
+
+def _fix_positions(work_x, join_dim):
+    u1 = jax.lax.axis_size("space")
+    ready = jnp.stack([work_x] * u1, axis=0)
+    z = jax.lax.all_to_all(ready, "space", 0, 0)
+    return jnp.concatenate(z, axis=join_dim)
+
+
+follow_object = functools.partial(_fix_positions, join_dim=0)
 
 
 def passed_along(block, axis, distance):
@@ -123,7 +134,7 @@
     hidden = jnp.where(before_f > 0, before_f, leak_slope * before_f).astype(jnp.bfloat16)
     grad_tile = lax.all_to_all(grad_out, "space", split_axis=1, concat_axis=4, tiled=True)[0]
     below = passed_along(hidden[-1:], "space", 1)
-    whole_weight = lax.all_gather(weight_two, "space", axis=0, tiled=True)
+    whole_weight = follow_object(weight_two)
     above = passed_along(grad_tile[:1], "space", -1)
     upper = jnp.pad(jnp.concatenate([grad_tile, above], axis=0), ((0, 0), (0, 1), (0, 1), (0, 0)))
     back = transpose_conv(upper, whole_weight)

time: 559 us -> 531 us (0.950); the launches traced: 558 us -> 523 us
  blocking collectives: 51.2 us -> 0 us
  starting transfers between devices: 24.2 us -> 35.1 us
    all_gather x1 -> x0, blocking collectives: 51.2 us -> none  [body(): whole_weight = lax.all_gather(weight_two, 'space', axis=0, tiled=True)]
    ppermute x2, waiting for transfers between devices: 1.76 us -> 13.6 us  [passed_along(): return lax.ppermute(block, axis, route)]
    all_to_all x0 -> x1, starting transfers between devices: none -> 10.2 us  [_fix_positions(): z = jax.lax.all_to_all(ready, 'space', 0, 0)]
    unnamed x3, waiting for transfers between devices: 234 us -> 226 us
    unnamed x71 -> x47, local copies, waits for them, and re-layouts: 11.9 us -> 13.4 us
  transfers between devices with their start and end apart: 7 -> 8, of which waited for: 3 -> 3; matrix products, arithmetic and copies ran while one was open for 14% -> 15% of each run, Pallas kernels for 0% -> 0%
where the time goes in v1:
time: 531 us; the launch traced here: 523 us
  waiting for transfers between devices  357 us (67%)
  local copies, waits for them, and re-layouts  58.6 us (11%)
  starting transfers between devices  35.1 us (7%)
  other arithmetic  30.2 us (6%)
  matrix products  26.3 us (5%)
  between operations  15.6 us (3%)
    unnamed x3, waiting for transfers between devices  226 us
    psum x1, waiting for transfers between devices, body(): coarse_all, fine_all = lax.psum((coarse_full, fine_full), 'dp')  118 us
    dot_general x9, matrix products, fine_terms(): lax.dot_general(flat_grad, piece, (((0,), (0,)), ((), ())), preferred_ele...  20.7 us
    ppermute x2, waiting for transfers between devices, passed_along(): return lax.ppermute(block, axis, route)  13.6 us
    unnamed x47, local copies, waits for them, and re-layouts  13.4 us
    all_to_all x1, starting transfers between devices, body(): lax.all_to_all(grad_out, 'space', split_axis=1, concat_axis=4, tiled=True)  11.7 us
  transfers between devices with their start and end apart: 8, of which 3 were waited for; matrix products, arithmetic and copies ran while one was open for 15% of the time, Pallas kernels for 0%

profile of v1, /device:TPU:1, one launch (start us, length us, event | category | flops | bytes accessed | tf_op | source)
XLA Modules:
  0.0 523.1 jit_solution(3914645068038190603)
XLA Ops:
  9.5 3.2 reshape.100
  12.7 11.7 %all-to-all-start = ((bf16[16,2,4096]{2,1,0:T(2,128)(2,1)}), bf16[16,2,4096]{2,1,0:T(2,128)(2,1)S(1)}, u32[]{:S(2)}, u32[]{:S(2)}) async-start(bf16[16,2,4096]{2,1,0:T(2,128)(2,1)} %reshape.100), calls=%async_computation | async-start | bytes 524288 | tf_op jit(solution)/shard_map/all_to_all | solution.py:135
  24.5 2.3 slice_bitcast_fusion.7
  26.7 5.0 collective-permute-start.1
  33.0 2.6 reshape.88
  35.6 2.8 fusion.22
  44.7 2.6 convert_bitcast_fusion
  48.5 10.2 %all-to-all-start.1 = ((bf16[16,8,3,3,3,128]{5,1,4,3,2,0:T(8,128)(2,1)}), bf16[16,8,3,3,3,128]{5,1,4,3,2,0:T(8,128)(2,1)}, u32[]{:S(2)}, u32[]{:S(2)}) async-start(bf16[16,8,3,3,3,128]{5,1,4,3,2,0:T(8,128)(2,1)} %stack.94), calls=%async_computation.1 | async-start | bytes 1769472 | tf_op jit(solution)/shard_map/all_to_all | solution.py:15
  61.5 3.6 reshape_squeeze.21
  71.1 4.6 select_maximum_fusion
  75.7 5.2 fusion.164
  80.9 9.0 %pad_maximum_fusion = bf16[6,66,32,384]{3,2,1,0:T(8,128)(2,1)} fusion(bf16[6,66,32,128]{3,2,1,0:T(8,128)(2,1)} %get-tuple-element.16, bf16[6,66,32,128]{3,2,1,0:T(8,128)(2,1)} %get-tuple-element.15, bf16[6,66,32,128]{3,2,1,0:T(8,128)(2,1)} %get-tuple-element.14), kind=kLoop, calls=%fused_computation.5 | loop fusion | flops 29196288 | bytes 19464192 | tf_op jit(solution)/shard_map/concatenate | solution.py:107
  89.8 13.6 %collective-permute-done = bf16[1,32,16,128]{1,3,2,0:T(8,128)(2,1)} collective-permute-done((bf16[1,32,16,128]{1,3,2,0:T(8,128)(2,1)S(1)}, bf16[1,32,16,128]{1,3,2,0:T(8,128)(2,1)}, u32[]{:S(2)}, u32[]{:S(2)}) %collective-permute-start) | collective-permute-done | bytes 131104 | tf_op jit(solution)/shard_map/ppermute | solution.py:25
  111.9 2.6 copy.72
  114.5 4.9 reshape.79
  119.4 3.4 multiply_convert_fusion
  122.8 2.2 fusion.96
  125.1 5.0 collective-permute-start.3
  130.1 4.9 fusion.45
  150.8 2.5 copy.73
  153.3 2.5 copy.74
  161.3 2.5 copy.75
  165.9 225.8 %all-reduce.23.cloned.1.call-done = (f32[128,3,3,3,128]{4,3,2,1,0:T(4,128)}, f32[128,3,3,3,128]{4,3,2,1,0:T(4,128)}) async-done(((f32[128,3,3,3,128]{4,3,2,1,0:T(4,128)}, f32[128,3,3,3,128]{4,3,2,1,0:T(4,128)}), (f32[128,3,3,3,128]{4,3,2,1,0:T(4,128)}, f32[128,3,3,3,128]{4,3,2,1,0:T(4,128)})) %all-reduce.23.cloned.1.call-update) | async-done | bytes 3538960
  394.9 117.9 %all-reduce.25.cloned.1.call-done = (f32[8,3,3,3,128]{4,3,2,1,0:T(4,128)}, f32[8,3,3,3,128]{4,3,2,1,0:T(4,128)}) async-done(((f32[8,3,3,3,128]{4,3,2,1,0:T(4,128)}, f32[8,3,3,3,128]{4,3,2,1,0:T(4,128)}), (f32[8,3,3,3,128]{4,3,2,1,0:T(4,128)}, f32[8,3,3,3,128]{4,3,2,1,0:T(4,128)})) %all-reduce.25.cloned.1.call-update) | async-done | bytes 221200 | tf_op jit(solution)/shard_map/psum | solution.py:146
  (121 shorter events, 56.8 us)
Async XLA Ops:
  7.2 1.2 copy-start
  9.5 23.5 %copy-start.2 = (bf16[1,4,64,32,128]{4,3,2,1,0:T(8,128)(2,1)S(1)}, bf16[1,4,64,32,128]{4,3,2,1,0:T(8,128)(2,1)}, u32[]{:S(2)}) copy-start(bf16[1,4,64,32,128]{4,3,2,1,0:T(8,128)(2,1)} %param.5) | copy-start | bytes 6291460
  12.7 34.7 %all-to-all-start = ((bf16[16,2,4096]{2,1,0:T(2,128)(2,1)}), bf16[16,2,4096]{2,1,0:T(2,128)(2,1)S(1)}, u32[]{:S(2)}, u32[]{:S(2)}) async-start(bf16[16,2,4096]{2,1,0:T(2,128)(2,1)} %reshape.100), calls=%async_computation | async-start | bytes 524288 | tf_op jit(solution)/shard_map/all_to_all | solution.py:135
  26.7 44.3 %collective-permute-start.1 = (bf16[1,64,32,128]{3,2,1,0:T(8,128)(2,1)}, bf16[1,64,32,128]{3,2,1,0:T(8,128)(2,1)}, u32[]{:S(2)}, u32[]{:S(2)}) collective-permute-start(bf16[1,64,32,128]{3,2,1,0:T(8,128)(2,1)} %get-tuple-element.19), channel_id=1, source_target_pairs={{0,1},{1,2},{2,3},{3,4},{4,5},{5,6},{6,7},{7,8},{8,9},{9,10},{10,1... | collective-permute-start | bytes 1572872 | tf_op jit(solution)/shard_map/ppermute | solution.py:35
  31.7 39.4 %collective-permute-start.2 = (bf16[1,64,32,128]{3,2,1,0:T(8,128)(2,1)}, bf16[1,64,32,128]{3,2,1,0:T(8,128)(2,1)}, u32[]{:S(2)}, u32[]{:S(2)}) collective-permute-start(bf16[1,64,32,128]{3,2,1,0:T(8,128)(2,1)} %get-tuple-element.20), channel_id=1, source_target_pairs={{1,0},{2,1},{3,2},{4,3},{5,4},{6,5},{7,6},{8,7},{9,8},{10,9},{11,1... | collective-permute-start | bytes 1572872 | tf_op jit(solution)/shard_map/ppermute | solution.py:36
  44.7 2.7 copy-start.13
  48.5 58.5 %all-to-all-start.1 = ((bf16[16,8,3,3,3,128]{5,1,4,3,2,0:T(8,128)(2,1)}), bf16[16,8,3,3,3,128]{5,1,4,3,2,0:T(8,128)(2,1)}, u32[]{:S(2)}, u32[]{:S(2)}) async-start(bf16[16,8,3,3,3,128]{5,1,4,3,2,0:T(8,128)(2,1)} %stack.94), calls=%async_computation.1 | async-start | bytes 1769472 | tf_op jit(solution)/shard_map/all_to_all | solution.py:15
  58.7 332.9 %all-reduce.23.cloned.1.call-start = ((), (), s32[]{:S(2)}) async-start(), calls=%async_computation.2 | async-start | bytes 9437184
  67.2 36.3 %collective-permute-start = (bf16[1,32,16,128]{1,3,2,0:T(8,128)(2,1)S(1)}, bf16[1,32,16,128]{1,3,2,0:T(8,128)(2,1)}, u32[]{:S(2)}, u32[]{:S(2)}) collective-permute-start(bf16[1,32,16,128]{1,3,2,0:T(8,128)(2,1)S(1)} %bitcast.333), channel_id=1, source_target_pairs={{1,0},{2,1},{3,2},{4,3},{5,4},{6,5},{7,6},{8,7},{9,8},{10,9},{11,1... | collective-permute-start | bytes 393224 | tf_op jit(solution)/shard_map/ppermute | solution.py:25
  109.4 1.2 copy-start.12
  109.5 1.6 copy-start.11
  114.5 4.9 copy-start.3
  119.4 15.7 %slice-start = ((s8[9732096]{0:T(1024)(128)(4,1)}), s8[1343488]{0:T(1024)(128)(4,1)S(1)}, s32[]{:S(2)}) async-start(s8[9732096]{0:T(1024)(128)(4,1)} %bitcast.312), calls=%async_computation.4 | async-start | bytes 2686976
  119.4 15.7 %slice-start.1 = ((s8[9732096]{0:T(1024)(128)(4,1)}), s8[4194304]{0:T(1024)(128)(4,1)S(1)}, s32[]{:S(2)}) async-start(s8[9732096]{0:T(1024)(128)(4,1)} %bitcast.312), calls=%async_computation.5 | async-start | bytes 8388608
  125.1 30.7 %collective-permute-start.3 = (bf16[1,64,32,128]{3,2,1,0:T(8,128)(2,1)}, bf16[1,64,32,128]{3,2,1,0:T(8,128)(2,1)S(1)}, u32[]{:S(2)}, u32[]{:S(2)}) collective-permute-start(bf16[1,64,32,128]{3,2,1,0:T(8,128)(2,1)} %fusion.96), channel_id=1, source_target_pairs={{0,1},{1,2},{2,3},{3,4},{4,5},{5,6},{6,7},{7,8},{8,9},{9,10},{10,1... | collective-permute-start | bytes 1572872 | tf_op jit(solution)/shard_map/ppermute | solution.py:25
  130.1 5.0 slice-start.2
  157.3 1.4 copy-start.9
  157.4 1.8 copy-start.7
  157.8 1.8 copy-start.6
  158.3 1.8 copy-start.8
  158.7 1.7 copy-start.5
  159.2 1.7 copy-start.4
  163.8 352.2 %copy-start.1 = (bf16[1,32,32,16,8]{2,4,3,1,0:T(8,128)(2,1)S(1)}, bf16[1,32,32,16,8]{2,4,3,1,0:T(8,128)(2,1)}, u32[]{:S(2)}) copy-start(bf16[1,32,32,16,8]{2,4,3,1,0:T(8,128)(2,1)} %param.7) | copy-start | bytes 786436
  163.9 348.9 %all-reduce.25.cloned.1.call-start = ((), (), s32[]{:S(2)}) async-start(), calls=%async_computation.3 | async-start | bytes 589824 | tf_op jit(solution)/shard_map/psum | solution.py:146
  (2 other events, 1.9 us)
Sparse Core Ops, SparseCore 0:
  164.0 227.6 all-reduce.22
  395.0 117.7 all-reduce.24
